TPU v7x, 512 devices: a whole 4x4x16 slice. The times are simulated.
512 devices in a mesh: ops: 16 (over x, y), sec: 32 (over z, core).
Axes of the slice: x: 4, y: 4, z: 16, core: 2. Of those that a mesh axis runs over, the one named last changes fastest.
Arguments:
- wave: bfloat16 [32, 768, 768], P('sec')
- left_ops: bfloat16 [16, 32, 768, 768], P('ops', 'sec'), may hold values from -0.21875 to 0.21875
- right_ops: bfloat16 [16, 32, 768, 768], P('ops', 'sec'), may hold values from -0.21875 to 0.21875
- priors: bfloat16 [8, 32, 768, 768], P(None, 'sec', 'ops'), as said below
- row_sizes: int32 [32], P('sec'), may hold values from 64 to 768, as said below
- col_sizes: int32 [32], P('sec'), may hold values from 64 to 768, as said below
Outputs:
- sigma: bfloat16 [32, 768, 768], P('sec', 'ops')
- new_dir: bfloat16 [32, 768, 768], P('sec', 'ops')
- correlations: float32 [8], replicated
Inputs may be any that keep to these rules, and one draw needn't show every extreme that they name: `row_sizes`: one sector's block uses all 768 rows. `col_sizes`: one sector's block uses all 768 columns. `priors`: each prior vector has a norm of about one over all cells.
All inputs are finite; a program needn't handle non-finite values.
Results may differ from a plain program's by a relative error of at most 0.012.
Values sent between devices are 32-bit elements; how exact they have to be, the bound alone decides.
No kernel may reach another device: no remote copies, remote signals or barrier semaphores. Data moves between devices by JAX's collectives and lax.ppermute only.
A program may use at most 64 MiB of HBM per device.

v0:
```python
import jax
import jax.numpy as jnp
from jax import lax
from jax.sharding import PartitionSpec as P


def shards(wave, left_ops, right_ops, priors, row_sizes, col_sizes):
    width = wave.shape[1]
    sec_local = wave.shape[0]
    shard_rows = width // lax.axis_size("ops")
    first_row = lax.axis_index("ops") * shard_rows
    place = jnp.arange(width, dtype=jnp.int32)
    row_mask = (place[None, :] < row_sizes[:, None]).astype(jnp.float32)
    col_mask = (place[None, :] < col_sizes[:, None]).astype(jnp.float32)
    full_mask = row_mask[:, :, None] * col_mask[:, None, :]
    masked = wave * full_mask.astype(jnp.bfloat16)
    inner = jnp.einsum(
        "sab,ksjb->ksaj", masked, right_ops, preferred_element_type=jnp.float32
    ).astype(jnp.bfloat16)
    partial_all = jnp.einsum("ksia,ksaj->sij", left_ops, inner, preferred_element_type=jnp.float32)
    whole = lax.psum(partial_all, "ops")
    summed = lax.dynamic_slice_in_dim(whole, first_row, shard_rows, 1)
    mine_rows = lax.dynamic_slice_in_dim(row_mask, first_row, shard_rows, 1)
    mine_mask = mine_rows[:, :, None] * col_mask[:, None, :]
    sigma = (summed * mine_mask).astype(jnp.bfloat16)
    pmask = (priors * mine_mask[None].astype(jnp.bfloat16)).astype(jnp.float32)
    sig32 = sigma.astype(jnp.float32)
    local_over = jnp.einsum("psab,sab->p", pmask, sig32, precision=lax.Precision.HIGHEST)
    correlations = lax.psum(local_over, ("ops", "sec"))
    resid = sig32 - jnp.einsum("p,psab->sab", correlations, pmask, precision=lax.Precision.HIGHEST)
    total = lax.psum(jnp.sum(resid * resid), ("ops", "sec"))
    cells = sec_local * lax.axis_size("sec") * width * width
    new_dir = (resid / jnp.sqrt(total / cells + 1e-06)).astype(jnp.bfloat16)
    return (sigma, new_dir, correlations)


def solution(mesh):
    in_specs = (
        P("sec", None, None),
        P("ops", "sec", None, None),
        P("ops", "sec", None, None),
        P(None, "sec", "ops", None),
        P("sec"),
        P("sec"),
    )
    out_specs = (P("sec", "ops", None), P("sec", "ops", None), P())
    return jax.shard_map(shards, mesh=mesh, in_specs=in_specs, out_specs=out_specs, check_vma=False)
```

profile of v0, /device:TPU:1, one launch (start us, length us, event | category | flops | bytes accessed | tf_op | source)
XLA Modules:
  0.0 362.4 jit_solution(13174631265643082113)
XLA Ops:
  7.2 0.0 copy-start
  7.2 0.0 all-reduce.2.cloned.1.call-start
  8.6 0.0 copy-done
  8.6 5.6 %convolution_bitcast_fusion = f32[1,768,768]{1,2,0:T(8,128)} fusion(bf16[1,1,768,768]{3,2,1,0:T(8,128)(2,1)S(1)} %copy-done, bf16[1,768,768]{2,1,0:T(8,128)(2,1)} %param.6, bf16[1,1,768,768]{3,2,1,0:T(8,128)(2,1)} %param.8, f32[768]{0:T(1024)S(1)} %get-tuple-element.7, f32[768]{0:T(1024)S(1)} %get-tuple-element.6), kind=kOutput, calls=%fused_computation.1 | convolution fusion | flops 1814298624 | bytes 5904384 | tf_op jit(solution)/shard_map/ksia,ksaj->sij/dot_general | solution.py:20
  14.2 0.0 copy-start.1
  14.2 0.0 all-reduce.2.cloned.1.call-update
  14.2 0.1 multiply_convert_fusion.2
  14.3 0.9 copy-done.1
  15.3 125.8 %all-reduce.2.cloned.1.call-done = f32[1,768,768]{1,2,0:T(8,128)} async-done(((f32[1,768,768]{1,2,0:T(8,128)}), f32[1,768,768]{1,2,0:T(8,128)}) %all-reduce.2.cloned.1.call-update) | async-done | bytes 2359312 | tf_op jit(solution)/shard_map/psum | solution.py:21
  141.1 1.4 fusion.19
  142.5 0.2 copy.12
  142.7 0.5 convolution_bitcast_fusion.1
  143.2 105.0 %psum.22 = f32[8]{0:T(128)S(1)} all-reduce(f32[8]{0:T(128)S(1)} %convolution_bitcast_fusion.1), channel_id=1, replica_groups=mesh['ops'=16,'sec'=32] {'ops','sec'}, use_global_device_ids=true, to_apply=%region_1.0 | all-reduce | flops 8 | bytes 64 | tf_op jit(solution)/shard_map/psum | solution.py:29
  248.2 0.0 copy-start.2
  248.2 0.6 fusion.11
  248.8 0.2 copy.13
  249.0 1.4 multiply_convert_fusion.1
  250.4 2.0 multiply_reduce_fusion
  252.4 0.0 copy-done.2
  252.4 0.8 copy.9
  253.2 99.5 %psum.23 = f32[]{:T(128)} all-reduce(f32[]{:T(128)} %multiply_reduce_fusion), channel_id=1, replica_groups=mesh['ops'=16,'sec'=32] {'ops','sec'}, use_global_device_ids=true, to_apply=%region_3.0 | all-reduce | flops 1 | bytes 8 | tf_op jit(solution)/shard_map/psum | solution.py:31
  353.4 1.4 divide_convert_fusion
  354.8 0.8 copy.10
  (3 shorter events, 0.1 us)
Async XLA Ops:
  7.2 1.5 copy-start
  7.2 133.9 %all-reduce.2.cloned.1.call-start = ((), (), s32[]{:S(2)}) async-start(), calls=%async_computation | async-start | bytes 4718592 | tf_op jit(solution)/shard_map/psum | solution.py:21
  14.2 1.1 copy-start.1
  248.2 4.3 %copy-start.2 = (f32[8]{0:T(128)}, f32[8]{0:T(128)S(1)}, u32[]{:S(2)}) copy-start(f32[8]{0:T(128)S(1)} %psum.22) | copy-start | bytes 100
Sparse Core Ops, SparseCore 0:
  14.3 126.6 all-reduce.1
where the time goes:
time: 363 us; the launch traced here: 362 us
  blocking collectives  204 us (56%)
  waiting for transfers between devices  126 us (35%)
  between operations  16.2 us (4%)
  matrix products  6.72 us (2%)
  other arithmetic  6.38 us (2%)
    psum x1, waiting for transfers between devices, shards(): whole = lax.psum(partial_all, 'ops')  126 us
    psum x1, blocking collectives, shards(): correlations = lax.psum(local_over, ('ops', 'sec'))  105 us
    psum x1, blocking collectives, shards(): total = lax.psum(jnp.sum(resid * resid), ('ops', 'sec'))  99.5 us
  transfers between devices with their start and end apart: 1, of which 1 were waited for; matrix products, arithmetic and copies ran while one was open for 0% of the time, Pallas kernels for 0%

commit v1 on v0

--- a/solution.py
+++ b/solution.py
@@ -18,7 +18,7 @@
         "sab,ksjb->ksaj", masked, right_ops, preferred_element_type=jnp.float32
     ).astype(jnp.bfloat16)
     partial_all = jnp.einsum("ksia,ksaj->sij", left_ops, inner, preferred_element_type=jnp.float32)
-    whole = lax.psum(partial_all, "ops")
+    whole = jnp.sum(lax.all_gather(partial_all, "ops"), axis=0)
     summed = lax.dynamic_slice_in_dim(whole, first_row, shard_rows, 1)
     mine_rows = lax.dynamic_slice_in_dim(row_mask, first_row, shard_rows, 1)
     mine_mask = mine_rows[:, :, None] * col_mask[:, None, :]

time: 363 us -> 510 us (1.40)
  waiting for transfers between devices: 126 us -> 239 us
  local copies, waits for them, and re-layouts: 2.84 us -> 24.1 us
  other arithmetic: 6.38 us -> 18.5 us
    all_gather x0 -> x1, waiting for transfers between devices: none -> 239 us  [shards(): whole = jnp.sum(lax.all_gather(partial_all, 'ops'), axis=0)]
    psum x1 -> x0, waiting for transfers between devices: 126 us -> none  [shards(): whole = lax.psum(partial_all, 'ops')]
    unnamed x8 -> x11, local copies, waits for them, and re-layouts: 2.47 us -> 23.6 us
    reduce_sum x0 -> x1, other arithmetic: none -> 16.2 us  [shards(): whole = jnp.sum(lax.all_gather(partial_all, 'ops'), axis=0)]
where the time goes in v1:
time: 510 us; the launch traced here: 509 us
  waiting for transfers between devices  239 us (47%)
  blocking collectives  204 us (40%)
  local copies, waits for them, and re-layouts  24.1 us (5%)
  other arithmetic  18.5 us (4%)
  between operations  16.2 us (3%)
  matrix products  6.73 us (1%)
    all_gather x1, waiting for transfers between devices, shards(): whole = jnp.sum(lax.all_gather(partial_all, 'ops'), axis=0)  239 us
    psum x1, blocking collectives, shards(): correlations = lax.psum(local_over, ('ops', 'sec'))  104 us
    psum x1, blocking collectives, shards(): total = lax.psum(jnp.sum(resid * resid), ('ops', 'sec'))  100 us
    unnamed x11, local copies, waits for them, and re-layouts  23.6 us
    reduce_sum x1, other arithmetic, shards(): whole = jnp.sum(lax.all_gather(partial_all, 'ops'), axis=0)  16.2 us
  transfers between devices with their start and end apart: 1, of which 1 were waited for; matrix products, arithmetic and copies ran while one was open for 0% of the time, Pallas kernels for 0%

profile of v1, /device:TPU:1, one launch (start us, length us, event | category | flops | bytes accessed | tf_op | source)
XLA Modules:
  0.0 509.0 jit_solution(15737355565459272287)
XLA Ops:
  7.2 0.0 copy-start
  7.2 0.0 all-gather.3.cloned.1.call-start
  8.6 0.0 copy-done
  8.6 5.6 %convolution_bitcast_fusion = f32[768,768]{0,1:T(8,128)} fusion(bf16[1,1,768,768]{3,2,1,0:T(8,128)(2,1)S(1)} %copy-done, bf16[1,768,768]{2,1,0:T(8,128)(2,1)} %param.6, bf16[1,1,768,768]{3,2,1,0:T(8,128)(2,1)} %param.8, f32[768]{0:T(1024)S(1)} %get-tuple-element.9, f32[768]{0:T(1024)S(1)} %get-tuple-element.8), kind=kOutput, calls=%fused_computation.2 | convolution fusion | flops 1814298624 | bytes 5904384 | tf_op jit(solution)/shard_map/ksia,ksaj->sij/dot_general | solution.py:20
  14.2 0.0 all-gather.3.cloned.1.call-update
  14.2 239.0 %all-gather.3.cloned.1.call-done = f32[12288,768]{0,1:T(8,128)} async-done(((f32[768,768]{0,1:T(8,128)}), f32[12288,768]{0,1:T(8,128)}) %all-gather.3.cloned.1.call-update) | async-done | bytes 37748752 | tf_op jit(solution)/shard_map/all_gather | solution.py:21
  253.2 22.0 %copy.15 = f32[96,8,16,768]{3,2,1,0:T(8,128)S(1)} copy(f32[96,8,16,768]{3,1,2,0:T(8,128)} %bitcast.54) | data formatting | bytes 75497472
  275.3 16.2 %bitcast_reduce_fusion = f32[768,768]{0,1:T(8,128)} fusion(f32[96,8,16,768]{3,2,1,0:T(8,128)S(1)} %copy.15), kind=kLoop, calls=%fused_computation | loop fusion | flops 8847360 | bytes 40108032 | tf_op jit(solution)/shard_map/reduce_sum | solution.py:21
  291.5 0.0 copy-start.2
  291.5 1.5 multiply_convert_fusion.1
  292.9 0.1 copy.9
  293.1 0.2 copy.13
  293.3 0.0 copy-done.2
  293.3 0.5 convolution_bitcast_fusion.1
  293.9 104.2 %psum.14 = f32[8]{0:T(128)S(1)} all-reduce(f32[8]{0:T(128)S(1)} %convolution_bitcast_fusion.1), channel_id=1, replica_groups=mesh['ops'=16,'sec'=32] {'ops','sec'}, use_global_device_ids=true, to_apply=%region_1.0 | all-reduce | flops 8 | bytes 64 | tf_op jit(solution)/shard_map/psum | solution.py:29
  398.0 0.0 copy-start.3
  398.0 0.0 copy-start.1
  398.0 0.6 fusion.11
  398.7 0.2 copy.14
  398.9 0.7 multiply_reduce_fusion
  399.6 0.8 copy.10
  400.3 100.3 %psum.15 = f32[]{:T(128)} all-reduce(f32[]{:T(128)} %multiply_reduce_fusion), channel_id=1, replica_groups=mesh['ops'=16,'sec'=32] {'ops','sec'}, use_global_device_ids=true, to_apply=%region_3.0 | all-reduce | flops 1 | bytes 8 | tf_op jit(solution)/shard_map/psum | solution.py:31
  501.3 0.1 fusion.15
  501.4 0.0 copy-done.3
  501.4 0.8 copy.11
  502.2 0.0 copy-done.1
  (3 shorter events, 0.1 us)
Async XLA Ops:
  7.2 1.5 copy-start
  7.2 246.1 %all-gather.3.cloned.1.call-start = ((), (), s32[]{:S(2)}) async-start(), calls=%async_computation | async-start | bytes 40108032 | tf_op jit(solution)/shard_map/all_gather | solution.py:21
  291.5 1.8 copy-start.2
  398.0 103.4 %copy-start.3 = (f32[8]{0:T(128)}, f32[8]{0:T(128)S(1)}, u32[]{:S(2)}) copy-start(f32[8]{0:T(128)S(1)} %psum.14) | copy-start | bytes 100
  398.0 104.2 %copy-start.1 = (bf16[1,1,768,768]{3,2,1,0:T(8,128)(2,1)S(1)}, bf16[1,1,768,768]{3,2,1,0:T(8,128)(2,1)}, u32[]{:S(2)}) copy-start(bf16[1,1,768,768]{3,2,1,0:T(8,128)(2,1)} %param.7) | copy-start | bytes 3538948
Sparse Core Ops, SparseCore 0:
  14.3 238.8 all-gather.2
